TPU v7x, 128 devices: a whole 4x4x4 slice. The times are simulated.
128 devices in a mesh: vx: 16 (over z, x), vy: 8 (over y, core).
Axes of the slice: x: 4, y: 4, z: 4, core: 2. Of those that a mesh axis runs over, the one named last changes fastest.
Arguments:
- fields: bfloat16 [4, 1024, 1280, 128], P(None, 'vx', 'vy'), may hold values from -6 to 6
- modulus: bfloat16 [1024, 1280, 128], P('vx', 'vy'), as said below
- anchors: int32 [16, 8, 14, 3], P('vx', 'vy'), may hold values from 0 to 10, as said below
- home_count: int32 [16, 8], P('vx', 'vy'), may hold values from 1 to 14, as said below
Outputs:
- gradient: float32 [1024, 1280, 128], P('vx', 'vy')
Inputs may be any that keep to these rules, and one draw needn't show every extreme that they name: `anchors`: column 0 is at most 4, column 1 at most 10, column 2 at most 2. `home_count`: the counts of the 16 tiles that share a vy index sum to 112. The modulus's real parts are positive and at least three times its imaginary parts, which are positive.
All inputs are finite; a program needn't handle non-finite values.
Results may differ from a plain program's by a relative error of at most 0.0003.
Values may be sent and summed in bfloat16 or wider, within the bound.
No kernel may reach another device: no remote copies, remote signals or barrier semaphores. Data moves between devices by JAX's collectives and lax.ppermute only.
A program may use at most 192 MiB of HBM per device.

v0:
```python
import jax
import jax.numpy as jnp
from jax import lax
from jax.sharding import PartitionSpec as P

NF = 4
SUB = 32
HALO = 16
TX = 64
TY = 160
RFWD = 3


OMEGA = 0.07


def with_halo(x, sides, width):
    for axis, dim in sides:
        size, length = (lax.axis_size(axis), x.shape[dim])
        up = [(i, (i + 1) % size) for i in range(size - 1)]
        down = [(j, i) for i, j in up]
        last = lax.slice_in_dim(x, length - width, length, axis=dim)
        first = lax.slice_in_dim(x, 0, width, axis=dim)
        before = lax.ppermute(last, axis, up)
        after = lax.ppermute(first, axis, down)
        x = jnp.concatenate([before, x, after], axis=dim)
    return x


def passed_along(x, axis, by):
    length = lax.axis_size(axis)
    pairs = [(i, i + by) for i in range(length) if 0 <= i + by < length]
    return lax.ppermute(x, axis, pairs)


def lane_shift(field, offset):
    width = field.shape[-1]
    if offset > 0:
        filler = jnp.zeros(field.shape[:-1] + (offset,), field.dtype)
        return jnp.concatenate([filler, field[..., : width - offset]], axis=-1)
    step = -offset
    filler = jnp.zeros(field.shape[:-1] + (step,), field.dtype)
    return jnp.concatenate([field[..., step:], filler], axis=-1)


def halves_swap(field):
    middle = field.shape[-1] // 2
    return jnp.concatenate([field[..., middle:], field[..., :middle]], axis=-1)


def laplace(field):
    lanes = field.shape[-1]
    depth = lax.broadcasted_iota(jnp.int32, (lanes,), 0) % (lanes // 2)
    padded = jnp.pad(field, ((0, 0), (1, 1), (1, 1), (0, 0)))
    beside = padded[:, 2:, 1:-1] + padded[:, :-2, 1:-1]
    beside = beside + padded[:, 1:-1, 2:] + padded[:, 1:-1, :-2]
    beside = beside + jnp.where(depth > 0, lane_shift(field, 1), 0.0)
    beside = beside + jnp.where(depth < lanes // 2 - 1, lane_shift(field, -1), 0.0)
    return 6.0 * field - beside


def cmul(left, right):
    lanes = left.shape[-1]
    upper = lax.broadcasted_iota(jnp.int32, (lanes,), 0) >= lanes // 2
    direct = left * right
    crossed = left * halves_swap(right)
    return jnp.where(upper, crossed + halves_swap(crossed), direct - halves_swap(direct))


def conjugate(value):
    lanes = value.shape[-1]
    upper = lax.broadcasted_iota(jnp.int32, (lanes,), 0) >= lanes // 2
    return jnp.where(upper, -value, value)


def subzone_grad(block):
    measured = block[:-1]
    stiff = block[-1:]
    lanes = block.shape[-1]
    present = jnp.max(stiff[0, :, :, : lanes // 2], axis=(0, 1)) > 0.0
    window = jnp.concatenate([present, present]).astype(jnp.float32)
    stiff_conj = conjugate(stiff)
    forward = jnp.zeros_like(measured)
    images = []
    for sweep in range(RFWD):
        image = laplace(forward)
        images.append(image)
        forward = (forward + OMEGA * (measured - forward - cmul(stiff, image))) * window
    adjoint = forward - measured
    result = jnp.zeros_like(measured[0])
    for sweep in range(RFWD - 1, 0, -1):
        result = result - OMEGA * jnp.sum(cmul(adjoint, conjugate(images[sweep])), axis=0)
        if sweep > 1:
            adjoint = (adjoint - OMEGA * (adjoint + laplace(cmul(stiff_conj, adjoint)))) * window
    return result


def shards(fields, modulus, anchors, home_count):
    data = jnp.concatenate([fields, modulus[None]], axis=0)
    extended = with_halo(data, (("vx", 1), ("vy", 2)), HALO)
    lanes = extended.shape[-1]
    spots = anchors[0, 0] * HALO
    count = home_count[0, 0]
    zero = jnp.zeros((), jnp.int32)
    lane_depth = lax.broadcasted_iota(jnp.int32, (lanes,), 0) % (lanes // 2)

    def extract(slot):
        corner = spots[slot]
        piece = lax.dynamic_slice(
            extended, (zero, corner[0], corner[1], zero), (NF + 1, SUB, SUB, lanes)
        )
        inside = (lane_depth >= corner[2]) & (lane_depth < corner[2] + SUB)
        return jnp.where(inside, piece, jnp.zeros_like(piece))

    def deposit(total, grad, slot):
        corner = spots[slot]
        start = (corner[0], corner[1], zero)
        current = lax.dynamic_slice(total, start, (SUB, SUB, lanes))
        return lax.dynamic_update_slice(total, current + grad, start)

    total = jnp.zeros((TX + 2 * HALO, TY + 2 * HALO, lanes), jnp.float32)

    def local_step(slot, total):
        return deposit(total, subzone_grad(extract(slot).astype(jnp.float32)), slot)

    total = lax.fori_loop(0, count, local_step, total)
    from_above = passed_along(total[:HALO], "vx", -1)
    from_below = passed_along(total[TX + HALO :], "vx", 1)
    middle = total[HALO : HALO + TX]
    middle = middle.at[:HALO].add(from_below).at[TX - HALO :].add(from_above)
    from_right = passed_along(middle[:, :HALO], "vy", -1)
    from_left = passed_along(middle[:, TY + HALO :], "vy", 1)
    owned = middle[:, HALO : HALO + TY]
    owned = owned.at[:, :HALO].add(from_left).at[:, TY - HALO :].add(from_right)
    return owned


def solution(mesh):
    return jax.shard_map(
        shards,
        mesh=mesh,
        in_specs=(
            P(None, "vx", "vy", None),
            P("vx", "vy", None),
            P("vx", "vy", None, None),
            P("vx", "vy"),
        ),
        out_specs=P("vx", "vy", None),
        check_vma=False,
    )
```

profile of v0, /device:TPU:7, one launch (start us, length us, event | category | flops | bytes accessed | tf_op | source)
XLA Modules:
  0.0 1216.9 jit_solution(2946076774029868015)
XLA Ops:
  9.3 68.3 %collective-permute-done = bf16[5,16,160,128]{3,2,1,0:T(8,128)(2,1)S(1)} collective-permute-done((bf16[5,16,160,128]{3,2,1,0:T(8,128)(2,1)S(1)}, bf16[5,16,160,128]{3,2,1,0:T(8,128)(2,1)S(1)}, u32[]{:S(2)}, u32[]{:S(2)}) %collective-permute-start) | collective-permute-done | bytes 3276832 | tf_op jit(solution)/shard_map/ppermute | solution.py:24
  77.6 5.3 collective-permute-done.1
  85.9 4.9 collective-permute-start.2
  92.7 19.9 %collective-permute-done.2 = bf16[5,96,16,128]{3,2,1,0:T(8,128)(2,1)} collective-permute-done((bf16[5,96,16,128]{3,2,1,0:T(8,128)(2,1)}, bf16[5,96,16,128]{3,2,1,0:T(8,128)(2,1)}, u32[]{:S(2)}, u32[]{:S(2)}) %collective-permute-start.2) | collective-permute-done | bytes 1966112 | tf_op jit(solution)/shard_map/ppermute | solution.py:24
  117.0 26.8 %pad_maximum_fusion = bf16[5,96,192,128]{3,2,1,0:T(8,128)(2,1)} fusion(bf16[5,96,16,128]{3,2,1,0:T(8,128)(2,1)} %collective-permute-done.3, bf16[5,16,160,128]{3,2,1,0:T(8,128)(2,1)} %copy-done.3, bf16[1,64,160,128]{3,2,1,0:T(8,128)(2,1)S(1)} %bitcast.24, bf16[4,64,160,128]{3,2,1,0:T(8,128)(2,1)} %param.14, bf16[5,16,160,128]{3,2,1,0:T(8,128)(2,1)} %copy-done.2, ...), kind=kLoop, calls=%fused_computation.103 | loop fusion | flops 141557760 | bytes 47185920 | tf_op jit(solution)/shard_map/concatenate | solution.py:26
  143.8 4.7 broadcast_in_dim.90
  148.5 515.7 %while.18 = (s32[]{:T(128)}, f32[96,192,128]{2,1,0:T(8,128)}, s32[]{:T(128)}, s32[14,3]{0,1:T(4,128)S(1)}, bf16[5,96,192,128]{3,2,1,0:T(8,128)(2,1)}, /*index=5*...) while((s32[]{:T(128)}, f32[96,192,128]{2,1,0:T(8,128)}, ...), condition=%wide.region_4.5_spmd.clone.clone, body=%wide.region_0.4_spmd.clone.clone.sunk | while | flops 63900428 | bytes 274965632 | solution.py:126
  199.3 5.2 fusion.119
  223.1 4.8 maximum_multiply_fusion.14
  268.8 5.2 fusion.119
  292.6 4.8 maximum_multiply_fusion.14
  339.0 5.2 fusion.119
  362.8 4.8 maximum_multiply_fusion.14
  409.2 5.2 fusion.119
  433.0 4.8 maximum_multiply_fusion.14
  479.4 5.2 fusion.119
  503.2 4.8 maximum_multiply_fusion.14
  549.4 5.2 fusion.119
  573.2 4.8 maximum_multiply_fusion.14
  618.9 5.2 fusion.119
  642.7 4.8 maximum_multiply_fusion.14
  670.9 16.0 %collective-permute-done.4 = f32[16,192,128]{2,1,0:T(8,128)S(1)} collective-permute-done((f32[16,192,128]{2,1,0:T(8,128)S(1)}, f32[16,192,128]{2,1,0:T(8,128)S(1)}, u32[]{:S(2)}, u32[]{:S(2)}) %collective-permute-start.4) | collective-permute-done | bytes 1572896 | tf_op jit(solution)/shard_map/ppermute | solution.py:33
  691.0 87.2 %collective-permute-done.5 = f32[16,192,128]{2,1,0:T(8,128)S(1)} collective-permute-done((f32[16,192,128]{2,1,0:T(8,128)S(1)}, f32[16,192,128]{2,1,0:T(8,128)S(1)}, u32[]{:S(2)}, u32[]{:S(2)}) %collective-permute-start.5) | collective-permute-done | bytes 1572896 | tf_op jit(solution)/shard_map/ppermute | solution.py:33
  778.7 425.7 %collective-permute-start.6 = (f32[64,16,128]{2,1,0:T(8,128)S(1)}, f32[64,16,128]{2,1,0:T(8,128)S(1)}, u32[]{:S(2)}, u32[]{:S(2)}) collective-permute-start(f32[64,16,128]{2,1,0:T(8,128)S(1)} %get-tuple-element.255), channel_id=1, source_target_pairs={{0,1},{1,2},{2,3},{3,4},{4,5},{5,6},{6,7},{8,9},{9,10},{10,11},{11... | collective-permute-start | bytes 1572872 | tf_op jit(solution)/shard_map/ppermute | solution.py:33
  (395 shorter events, 423.0 us)
Async XLA Ops:
  0.0 82.9 %slice-start = ((s8[10485760]{0:T(1024)(128)(4,1)}), s8[4194304]{0:T(1024)(128)(4,1)S(1)}, s32[]{:S(2)}) async-start(s8[10485760]{0:T(1024)(128)(4,1)} %bitcast.20), calls=%async_computation | async-start | bytes 8388608
  0.0 82.9 %slice-start.1 = ((s8[10485760]{0:T(1024)(128)(4,1)}), s8[4194304]{0:T(1024)(128)(4,1)S(1)}, s32[]{:S(2)}) async-start(s8[10485760]{0:T(1024)(128)(4,1)} %bitcast.20), calls=%async_computation.1 | async-start | bytes 8388608
  0.0 82.9 %slice-start.2 = ((s8[10485760]{0:T(1024)(128)(4,1)}), s8[2097152]{0:T(1024)(128)(4,1)S(1)}, s32[]{:S(2)}) async-start(s8[10485760]{0:T(1024)(128)(4,1)} %bitcast.20), calls=%async_computation.2 | async-start | bytes 4194304
  0.0 82.9 %copy-start.1 = (bf16[64,160,128]{2,1,0:T(8,128)(2,1)S(1)}, bf16[64,160,128]{2,1,0:T(8,128)(2,1)}, u32[]{:S(2)}) copy-start(bf16[64,160,128]{2,1,0:T(8,128)(2,1)} %param.15) | copy-start | bytes 7864324
  3.6 74.0 %collective-permute-start = (bf16[5,16,160,128]{3,2,1,0:T(8,128)(2,1)S(1)}, bf16[5,16,160,128]{3,2,1,0:T(8,128)(2,1)S(1)}, u32[]{:S(2)}, u32[]{:S(2)}) collective-permute-start(bf16[5,16,160,128]{3,2,1,0:T(8,128)(2,1)S(1)} %get-tuple-element.250), channel_id=1, source_target_pairs={{0,8},{8,16},{16,24},{24,32},{32,40},{40,48},{48,56},{56,64},{64,7... | collective-permute-start | bytes 9830408 | tf_op jit(solution)/shard_map/ppermute | solution.py:24
  7.3 85.3 %copy-start.5 = (s32[1,1,14,3]{2,1,3,0:T(1,128)S(1)}, s32[1,1,14,3]{2,1,3,0:T(1,128)}, u32[]{:S(2)}) copy-start(s32[1,1,14,3]{2,1,3,0:T(1,128)} %param.16) | copy-start | bytes 508
  7.4 75.5 %collective-permute-start.1 = (bf16[5,16,160,128]{3,2,1,0:T(8,128)(2,1)S(1)}, bf16[5,16,160,128]{3,2,1,0:T(8,128)(2,1)S(1)}, u32[]{:S(2)}, u32[]{:S(2)}) collective-permute-start(bf16[5,16,160,128]{3,2,1,0:T(8,128)(2,1)S(1)} %get-tuple-element.251), channel_id=1, source_target_pairs={{8,0},{16,8},{24,16},{32,24},{40,32},{48,40},{56,48},{64,56},{72,6... | collective-permute-start | bytes 9830408 | tf_op jit(solution)/shard_map/ppermute | solution.py:25
  77.6 8.3 copy-start.2
  82.9 2.9 copy-start.3
  85.9 26.8 %collective-permute-start.2 = (bf16[5,96,16,128]{3,2,1,0:T(8,128)(2,1)}, bf16[5,96,16,128]{3,2,1,0:T(8,128)(2,1)}, u32[]{:S(2)}, u32[]{:S(2)}) collective-permute-start(bf16[5,96,16,128]{3,2,1,0:T(8,128)(2,1)} %get-tuple-element.248), channel_id=1, source_target_pairs={{0,1},{1,2},{2,3},{3,4},{4,5},{5,6},{6,7},{8,9},{9,10},{10,11},{11... | collective-permute-start | bytes 5898248 | tf_op jit(solution)/shard_map/ppermute | solution.py:24
  90.8 26.3 %collective-permute-start.3 = (bf16[5,96,16,128]{3,2,1,0:T(8,128)(2,1)}, bf16[5,96,16,128]{3,2,1,0:T(8,128)(2,1)}, u32[]{:S(2)}, u32[]{:S(2)}) collective-permute-start(bf16[5,96,16,128]{3,2,1,0:T(8,128)(2,1)} %get-tuple-element.249), channel_id=1, source_target_pairs={{1,0},{2,1},{3,2},{4,3},{5,4},{6,5},{7,6},{9,8},{10,9},{11,10},{12... | collective-permute-start | bytes 5898248 | tf_op jit(solution)/shard_map/ppermute | solution.py:25
  220.3 2.8 copy-start
  289.9 2.8 copy-start
  360.1 2.8 copy-start
  430.2 2.8 copy-start
  500.4 2.8 copy-start
  570.5 2.8 copy-start
  640.0 2.8 copy-start
  665.7 21.2 %collective-permute-start.4 = (f32[16,192,128]{2,1,0:T(8,128)S(1)}, f32[16,192,128]{2,1,0:T(8,128)S(1)}, u32[]{:S(2)}, u32[]{:S(2)}) collective-permute-start(f32[16,192,128]{2,1,0:T(8,128)S(1)} %slice.525), channel_id=1, source_target_pairs={{0,8},{8,16},{16,24},{24,32},{32,40},{40,48},{48,56},{56,64},{64,7... | collective-permute-start | bytes 4718600 | tf_op jit(solution)/shard_map/ppermute | solution.py:33
  689.1 89.1 %collective-permute-start.5 = (f32[16,192,128]{2,1,0:T(8,128)S(1)}, f32[16,192,128]{2,1,0:T(8,128)S(1)}, u32[]{:S(2)}, u32[]{:S(2)}) collective-permute-start(f32[16,192,128]{2,1,0:T(8,128)S(1)} %get-tuple-element.252), channel_id=1, source_target_pairs={{8,0},{16,8},{24,16},{32,24},{40,32},{48,40},{56,48},{64,56},{72,6... | collective-permute-start | bytes 4718600 | tf_op jit(solution)/shard_map/ppermute | solution.py:33
  778.7 431.8 %collective-permute-start.6 = (f32[64,16,128]{2,1,0:T(8,128)S(1)}, f32[64,16,128]{2,1,0:T(8,128)S(1)}, u32[]{:S(2)}, u32[]{:S(2)}) collective-permute-start(f32[64,16,128]{2,1,0:T(8,128)S(1)} %get-tuple-element.255), channel_id=1, source_target_pairs={{0,1},{1,2},{2,3},{3,4},{4,5},{5,6},{6,7},{8,9},{9,10},{10,11},{11... | collective-permute-start | bytes 1572872 | tf_op jit(solution)/shard_map/ppermute | solution.py:33
  1204.3 10.5 collective-permute-start.7
  1210.5 4.3 copy-start.4
where the time goes:
time: 1230 us; the launch traced here: 1220 us
  starting transfers between devices  444 us (36%)
  other arithmetic  282 us (23%)
  local copies, waits for them, and re-layouts  217 us (18%)
  waiting for transfers between devices  209 us (17%)
  loops' own time  64.9 us (5%)
    ppermute x4, starting transfers between devices, passed_along(): return lax.ppermute(x, axis, pairs)  431 us
    slice x126, local copies, waits for them, and re-layouts, halves_swap(): return jnp.concatenate([field[..., middle:], field[..., :middle]], axis=-1)  131 us
    ppermute x4, waiting for transfers between devices, passed_along(): return lax.ppermute(x, axis, pairs)  111 us
    ppermute x2, waiting for transfers between devices, with_halo(): before = lax.ppermute(last, axis, up)  88.2 us
    another operation x1, loops' own time, shards(): total = lax.fori_loop(0, count, local_step, total)  64.9 us
    mul x35, other arithmetic, cmul(): direct = left * right  61 us
    mul x21, other arithmetic, subzone_grad(): (forward + OMEGA * (measured - forward - cmul(stiff, image))) * window  57.8 us
    mul x42, other arithmetic, cmul(): crossed = left * halves_swap(right)  52.5 us
  transfers between devices with their start and end apart: 8, of which 8 were waited for; matrix products, arithmetic and copies ran while one was open for 0% of the time, Pallas kernels for 0%

commit v1 on v0

v1 whole, which is shorter than its diff:
```python
import functools

import jax
import jax.numpy as jnp
from jax import lax
from jax.experimental import pallas as pl
from jax.experimental.pallas import tpu as pltpu
from jax.sharding import PartitionSpec as P

NF = 4
SUB = 32
HALO = 16
TX = 64
TY = 160
RFWD = 3


OMEGA = 0.07
PADY = 8


def with_halo(x, sides, width):
    for axis, dim in sides:
        size, length = (lax.axis_size(axis), x.shape[dim])
        up = [(i, (i + 1) % size) for i in range(size - 1)]
        down = [(j, i) for i, j in up]
        last = lax.slice_in_dim(x, length - width, length, axis=dim)
        first = lax.slice_in_dim(x, 0, width, axis=dim)
        before = lax.ppermute(last, axis, up)
        after = lax.ppermute(first, axis, down)
        x = jnp.concatenate([before, x, after], axis=dim)
    return x


def passed_along(x, axis, by):
    length = lax.axis_size(axis)
    pairs = [(i, i + by) for i in range(length) if 0 <= i + by < length]
    return lax.ppermute(x, axis, pairs)


def subzone_kernel(spots_ref, count_ref, block_ref, total_ref,
                   um_ref, mur_ref, muis_ref, w1_ref, w2_ref, t_ref,
                   img1_ref, s1_ref, v3_ref, p_ref, q_ref):
    slot = pl.program_id(0)
    lanes = block_ref.shape[-1]
    half = lanes // 2

    @pl.when(slot == 0)
    def _():
        total_ref[...] = jnp.zeros_like(total_ref)
        w1_ref[...] = jnp.zeros_like(w1_ref)
        w2_ref[...] = jnp.zeros_like(w2_ref)
        t_ref[...] = jnp.zeros_like(t_ref)

    @pl.when(slot < count_ref[0])
    def _():
        x0 = spots_ref[slot, 0]
        y0 = pl.multiple_of(spots_ref[slot, 1], HALO)
        z0 = spots_ref[slot, 2]
        lane = lax.broadcasted_iota(jnp.int32, (SUB, lanes), 1)
        depth = lane % half
        window = (depth >= z0) & (depth < z0 + SUB)
        upper = lane >= half

        def swap(v):
            return pltpu.roll(v, half, 1)

        def laplace(ref, f, x):
            c = ref[f, x + 1, PADY:PADY + SUB, :]
            side = ref[f, x, PADY:PADY + SUB, :] + ref[f, x + 2, PADY:PADY + SUB, :]
            side = side + ref[f, x + 1, PADY - 1:PADY - 1 + SUB, :]
            side = side + ref[f, x + 1, PADY + 1:PADY + 1 + SUB, :]
            side = side + pltpu.roll(c, 1, 1) + pltpu.roll(c, lanes - 1, 1)
            return 6.0 * c - side, c

        def stage_a(x, carry):
            mu = jnp.where(window, block_ref[NF, x].astype(jnp.float32), 0.0)
            smu = swap(mu)
            mur_ref[x] = jnp.where(upper, smu, mu)
            muis_ref[x] = jnp.where(upper, mu, -smu)
            for f in range(NF):
                u = jnp.where(window, block_ref[f, x].astype(jnp.float32), 0.0)
                um_ref[f, x] = u
                w1_ref[f, x + 1, PADY:PADY + SUB, :] = OMEGA * u
            return carry

        lax.fori_loop(0, SUB, stage_a, 0)

        def stage_b(x, carry):
            mur = mur_ref[x]
            muis = muis_ref[x]
            for f in range(NF):
                img, c = laplace(w1_ref, f, x)
                s = swap(img)
                u = um_ref[f, x]
                w2_ref[f, x + 1, PADY:PADY + SUB, :] = c + OMEGA * (u - c - (mur * img + muis * s))
                img1_ref[f, x] = img
                s1_ref[f, x] = s
            return carry

        lax.fori_loop(0, SUB, stage_b, 0)

        def stage_c(x, carry):
            mur = mur_ref[x]
            muis = muis_ref[x]
            pacc = jnp.zeros((SUB, lanes), jnp.float32)
            qacc = jnp.zeros((SUB, lanes), jnp.float32)
            for f in range(NF):
                img, c = laplace(w2_ref, f, x)
                s = swap(img)
                u = um_ref[f, x]
                w3 = c + OMEGA * (u - c - (mur * img + muis * s))
                v3 = w3 - u
                t_ref[f, x + 1, PADY:PADY + SUB, :] = mur * v3 - muis * swap(v3)
                v3_ref[f, x] = v3
                pacc = pacc + v3 * img
                qacc = qacc + v3 * s
            p_ref[x] = pacc
            q_ref[x] = qacc
            return carry

        lax.fori_loop(0, SUB, stage_c, 0)

        def stage_d(x, carry):
            pacc = p_ref[x]
            qacc = q_ref[x]
            for f in range(NF):
                lt, _ = laplace(t_ref, f, x)
                v3 = v3_ref[f, x]
                v2 = v3 - OMEGA * (v3 + lt)
                pacc = pacc + v2 * img1_ref[f, x]
                qacc = qacc + v2 * s1_ref[f, x]
            res = jnp.where(upper, qacc - swap(qacc), pacc + swap(pacc))
            res = jnp.where(window, -OMEGA * res, 0.0)
            total_ref[x0 + x, pl.ds(y0, SUB), :] += res
            return carry

        lax.fori_loop(0, SUB, stage_d, 0)


def subzone_pass(extended, spots, count):
    lanes = extended.shape[-1]
    home = spots.shape[0]
    ex, ey = extended.shape[1], extended.shape[2]

    def block_map(s, spots_ref, count_ref):
        live = jnp.minimum(s, jnp.maximum(count_ref[0] - 1, 0))
        return (0, spots_ref[live, 0], pl.multiple_of(spots_ref[live, 1], HALO), 0)

    f32 = jnp.float32
    padded = (NF, SUB + 2, SUB + 2 * PADY, lanes)
    grid_spec = pltpu.PrefetchScalarGridSpec(
        num_scalar_prefetch=2,
        grid=(home,),
        in_specs=[pl.BlockSpec((pl.Element(NF + 1), pl.Element(SUB), pl.Element(SUB), pl.Element(lanes)), block_map)],
        out_specs=pl.BlockSpec((ex, ey, lanes), lambda s, spots_ref, count_ref: (0, 0, 0)),
        scratch_shapes=[
            pltpu.VMEM((NF, SUB, SUB, lanes), f32),
            pltpu.VMEM((SUB, SUB, lanes), f32),
            pltpu.VMEM((SUB, SUB, lanes), f32),
            pltpu.VMEM(padded, f32),
            pltpu.VMEM(padded, f32),
            pltpu.VMEM(padded, f32),
            pltpu.VMEM((NF, SUB, SUB, lanes), f32),
            pltpu.VMEM((NF, SUB, SUB, lanes), f32),
            pltpu.VMEM((NF, SUB, SUB, lanes), f32),
            pltpu.VMEM((SUB, SUB, lanes), f32),
            pltpu.VMEM((SUB, SUB, lanes), f32),
        ],
    )
    return pl.pallas_call(
        subzone_kernel,
        grid_spec=grid_spec,
        out_shape=jax.ShapeDtypeStruct((ex, ey, lanes), f32),
        compiler_params=pltpu.CompilerParams(
            dimension_semantics=("arbitrary",), vmem_limit_bytes=100 * 1024 * 1024
        ),
    )(spots, count, extended)


def shards(fields, modulus, anchors, home_count):
    data = jnp.concatenate([fields, modulus[None]], axis=0)
    extended = with_halo(data, (("vx", 1), ("vy", 2)), HALO)
    spots = (anchors[0, 0] * HALO).astype(jnp.int32)
    count = home_count[0].astype(jnp.int32)
    total = subzone_pass(extended, spots, count)
    from_above = passed_along(total[:HALO], "vx", -1)
    from_below = passed_along(total[TX + HALO :], "vx", 1)
    middle = total[HALO : HALO + TX]
    middle = middle.at[:HALO].add(from_below).at[TX - HALO :].add(from_above)
    from_right = passed_along(middle[:, :HALO], "vy", -1)
    from_left = passed_along(middle[:, TY + HALO :], "vy", 1)
    owned = middle[:, HALO : HALO + TY]
    owned = owned.at[:, :HALO].add(from_left).at[:, TY - HALO :].add(from_right)
    return owned


def solution(mesh):
    return jax.shard_map(
        shards,
        mesh=mesh,
        in_specs=(
            P(None, "vx", "vy", None),
            P("vx", "vy", None),
            P("vx", "vy", None, None),
            P("vx", "vy"),
        ),
        out_specs=P("vx", "vy", None),
        check_vma=False,
    )
```

time: 1230 us -> 510 us (0.41)
  starting transfers between devices: 444 us -> 22.6 us
  Pallas kernels: 0 us -> 316 us
  other arithmetic: 282 us -> 35.8 us
  local copies, waits for them, and re-layouts: 217 us -> 3.43 us
  waiting for transfers between devices: 209 us -> 124 us
  loops' own time: 64.9 us -> 0 us
    ppermute x4, starting transfers between devices: 431 us -> 10.2 us  [passed_along(): return lax.ppermute(x, axis, pairs)]
    pallas_call x0 -> x1, Pallas kernels: none -> 316 us  [subzone_pass(): pl.pallas_call(subzone_kernel, grid_spec=grid_spec, out_shape=jax.ShapeDt...]
    slice x155 -> x1, local copies, waits for them, and re-layouts: 181 us -> 2.24 us  [shards(): from_above = passed_along(total[:HALO], 'vx', -1)]
    mul x99 -> x1, other arithmetic: 171 us -> 0.01 us  [shards(): spots = (anchors[0, 0] * HALO).astype(jnp.int32)]
    ppermute x4, waiting for transfers between devices: 111 us -> 27.3 us  [passed_along(): return lax.ppermute(x, axis, pairs)]
    another operation x1 -> x0, loops' own time: 64.9 us -> none  [shards(): total = lax.fori_loop(0, count, local_step, total)]
    dynamic_update_slice x7 -> x0, local copies, waits for them, and re-layouts: 25.3 us -> none  [deposit(): return lax.dynamic_update_slice(total, current + grad, start)]
    reduce_sum x7 -> x0, other arithmetic: 22.6 us -> none  [subzone_grad(): jnp.sum(cmul(adjoint, conjugate(images[sweep])), axis=0)]
where the time goes in v1:
time: 510 us; the launch traced here: 503 us
  Pallas kernels  316 us (62%)
  waiting for transfers between devices  124 us (24%)
  other arithmetic  35.8 us (7%)
  starting transfers between devices  22.6 us (4%)
    pallas_call x1, Pallas kernels, subzone_pass(): pl.pallas_call(subzone_kernel, grid_spec=grid_spec, out_shape=jax.ShapeDt...  316 us
    ppermute x2, waiting for transfers between devices, with_halo(): before = lax.ppermute(last, axis, up)  86.9 us
    ppermute x4, waiting for transfers between devices, passed_along(): return lax.ppermute(x, axis, pairs)  27.3 us
    concatenate x1, other arithmetic, with_halo(): x = jnp.concatenate([before, x, after], axis=dim)  26.8 us
  transfers between devices with their start and end apart: 8, of which 8 were waited for; matrix products, arithmetic and copies ran while one was open for 0% of the time, Pallas kernels for 0%

profile of v1, /device:TPU:7, one launch (start us, length us, event | category | flops | bytes accessed | tf_op | source)
XLA Modules:
  0.0 502.8 jit_solution(3555891087463482725)
XLA Ops:
  0.0 3.6 pad_maximum_fusion.2
  3.6 3.7 collective-permute-start
  7.4 1.9 collective-permute-start.1
  9.3 68.3 %collective-permute-done = bf16[5,16,160,128]{3,2,1,0:T(8,128)(2,1)S(1)} collective-permute-done((bf16[5,16,160,128]{3,2,1,0:T(8,128)(2,1)S(1)}, bf16[5,16,160,128]{3,2,1,0:T(8,128)(2,1)S(1)}, u32[]{:S(2)}, u32[]{:S(2)}) %collective-permute-start) | collective-permute-done | bytes 3276832 | tf_op jit(solution)/shard_map/ppermute | solution.py:29
  77.6 5.3 %collective-permute-done.1 = bf16[5,16,160,128]{3,2,1,0:T(8,128)(2,1)S(1)} collective-permute-done((bf16[5,16,160,128]{3,2,1,0:T(8,128)(2,1)S(1)}, bf16[5,16,160,128]{3,2,1,0:T(8,128)(2,1)S(1)}, u32[]{:S(2)}, u32[]{:S(2)}) %collective-permute-start.1) | collective-permute-done | bytes 3276832 | tf_op jit(solution)/shard_map/ppermute | solution.py:30
  82.9 2.9 pad_maximum_fusion.6
  85.8 4.9 collective-permute-start.2
  90.7 1.9 collective-permute-start.3
  92.7 0.7 copy.6
  94.0 18.6 %collective-permute-done.2 = bf16[5,96,16,128]{3,2,1,0:T(8,128)(2,1)} collective-permute-done((bf16[5,96,16,128]{3,2,1,0:T(8,128)(2,1)}, bf16[5,96,16,128]{3,2,1,0:T(8,128)(2,1)}, u32[]{:S(2)}, u32[]{:S(2)}) %collective-permute-start.2) | collective-permute-done | bytes 1966112 | tf_op jit(solution)/shard_map/ppermute | solution.py:29
  112.6 4.4 collective-permute-done.3
  117.0 26.8 %pad_maximum_fusion.block_ref = bf16[5,96,192,128]{3,2,1,0:T(8,128)(2,1)} fusion(bf16[5,96,16,128]{3,2,1,0:T(8,128)(2,1)} %collective-permute-done.3, bf16[5,16,160,128]{3,2,1,0:T(8,128)(2,1)} %copy-done.3, bf16[1,64,160,128]{3,2,1,0:T(8,128)(2,1)S(1)} %bitcast.8, bf16[4,64,160,128]{3,2,1,0:T(8,128)(2,1)} %param.12, bf16[5,16,160,128]{3,2,1,0:T(8,128)(2,1)} %copy-done.2, ...), kind=kLoop, calls=%fused_computation | loop fusion | flops 141557760 | bytes 47185920 | tf_op jit(solution)/shard_map/concatenate | solution.py:31
  143.8 316.2 %shard_map.46 = f32[96,192,128]{2,1,0:T(8,128)} custom-call(s32[14,3]{1,0:T(8,128)} %bitcast.9, s32[1]{0:T(128)} %bitcast.3.count_ref, bf16[5,96,192,128]{3,2,1,0:T(8,128)(2,1)} %pad_maximum_fusion.block_ref), custom_call_target="tpu_custom_call" | custom-call | tf_op jit(solution)/shard_map/pallas_call | solution.py:171
  460.0 2.2 fusion.4
  462.2 2.2 collective-permute-start.4
  464.4 3.6 collective-permute-start.5
  468.1 15.6 %collective-permute-done.4 = f32[16,192,128]{2,1,0:T(8,128)S(1)} collective-permute-done((f32[16,192,128]{2,1,0:T(8,128)S(1)}, f32[16,192,128]{2,1,0:T(8,128)S(1)}, u32[]{:S(2)}, u32[]{:S(2)}) %collective-permute-start.4) | collective-permute-done | bytes 1572896 | tf_op jit(solution)/shard_map/ppermute | solution.py:38
  483.8 4.1 collective-permute-done.5
  488.0 0.4 fusion
  488.4 1.9 collective-permute-start.6
  490.3 2.4 collective-permute-start.7
  493.1 3.3 collective-permute-done.6
  496.6 4.3 collective-permute-done.7
  500.9 1.9 fusion.2
  (26 shorter events, 0.8 us)
Async XLA Ops:
  0.0 82.9 %slice-start = ((s8[10485760]{0:T(1024)(128)(4,1)}), s8[4194304]{0:T(1024)(128)(4,1)S(1)}, s32[]{:S(2)}) async-start(s8[10485760]{0:T(1024)(128)(4,1)} %bitcast.4), calls=%async_computation | async-start | bytes 8388608
  0.0 82.9 %slice-start.1 = ((s8[10485760]{0:T(1024)(128)(4,1)}), s8[4194304]{0:T(1024)(128)(4,1)S(1)}, s32[]{:S(2)}) async-start(s8[10485760]{0:T(1024)(128)(4,1)} %bitcast.4), calls=%async_computation.1 | async-start | bytes 8388608
  0.0 82.9 %slice-start.2 = ((s8[10485760]{0:T(1024)(128)(4,1)}), s8[2097152]{0:T(1024)(128)(4,1)S(1)}, s32[]{:S(2)}) async-start(s8[10485760]{0:T(1024)(128)(4,1)} %bitcast.4), calls=%async_computation.2 | async-start | bytes 4194304
  0.0 82.9 %copy-start.1 = (bf16[64,160,128]{2,1,0:T(8,128)(2,1)S(1)}, bf16[64,160,128]{2,1,0:T(8,128)(2,1)}, u32[]{:S(2)}) copy-start(bf16[64,160,128]{2,1,0:T(8,128)(2,1)} %param.13) | copy-start | bytes 7864324
  3.6 74.0 %collective-permute-start = (bf16[5,16,160,128]{3,2,1,0:T(8,128)(2,1)S(1)}, bf16[5,16,160,128]{3,2,1,0:T(8,128)(2,1)S(1)}, u32[]{:S(2)}, u32[]{:S(2)}) collective-permute-start(bf16[5,16,160,128]{3,2,1,0:T(8,128)(2,1)S(1)} %get-tuple-element.55), channel_id=1, source_target_pairs={{0,8},{8,16},{16,24},{24,32},{32,40},{40,48},{48,56},{56,64},{64,7... | collective-permute-start | bytes 9830408 | tf_op jit(solution)/shard_map/ppermute | solution.py:29
  7.3 85.3 %copy-start.5 = (s32[1,1,14,3]{2,1,3,0:T(1,128)S(1)}, s32[1,1,14,3]{2,1,3,0:T(1,128)}, u32[]{:S(2)}) copy-start(s32[1,1,14,3]{2,1,3,0:T(1,128)} %param.14) | copy-start | bytes 508
  7.4 75.5 %collective-permute-start.1 = (bf16[5,16,160,128]{3,2,1,0:T(8,128)(2,1)S(1)}, bf16[5,16,160,128]{3,2,1,0:T(8,128)(2,1)S(1)}, u32[]{:S(2)}, u32[]{:S(2)}) collective-permute-start(bf16[5,16,160,128]{3,2,1,0:T(8,128)(2,1)S(1)} %get-tuple-element.56), channel_id=1, source_target_pairs={{8,0},{16,8},{24,16},{32,24},{40,32},{48,40},{56,48},{64,56},{72,6... | collective-permute-start | bytes 9830408 | tf_op jit(solution)/shard_map/ppermute | solution.py:30
  77.6 8.2 %copy-start.2 = (bf16[5,16,160,128]{3,2,1,0:T(8,128)(2,1)}, bf16[5,16,160,128]{3,2,1,0:T(8,128)(2,1)S(1)}, u32[]{:S(2)}) copy-start(bf16[5,16,160,128]{3,2,1,0:T(8,128)(2,1)S(1)} %collective-permute-done) | copy-start | bytes 9830404
  82.9 2.9 copy-start.3
  85.8 26.8 %collective-permute-start.2 = (bf16[5,96,16,128]{3,2,1,0:T(8,128)(2,1)}, bf16[5,96,16,128]{3,2,1,0:T(8,128)(2,1)}, u32[]{:S(2)}, u32[]{:S(2)}) collective-permute-start(bf16[5,96,16,128]{3,2,1,0:T(8,128)(2,1)} %get-tuple-element.53), channel_id=1, source_target_pairs={{0,1},{1,2},{2,3},{3,4},{4,5},{5,6},{6,7},{8,9},{9,10},{10,11},{11... | collective-permute-start | bytes 5898248 | tf_op jit(solution)/shard_map/ppermute | solution.py:29
  90.7 26.3 %collective-permute-start.3 = (bf16[5,96,16,128]{3,2,1,0:T(8,128)(2,1)}, bf16[5,96,16,128]{3,2,1,0:T(8,128)(2,1)}, u32[]{:S(2)}, u32[]{:S(2)}) collective-permute-start(bf16[5,96,16,128]{3,2,1,0:T(8,128)(2,1)} %get-tuple-element.54), channel_id=1, source_target_pairs={{1,0},{2,1},{3,2},{4,3},{5,4},{6,5},{7,6},{9,8},{10,9},{11,10},{12... | collective-permute-start | bytes 5898248 | tf_op jit(solution)/shard_map/ppermute | solution.py:30
  460.0 23.7 %copy-start = (f32[96,192,128]{2,1,0:T(8,128)S(1)}, f32[96,192,128]{2,1,0:T(8,128)}, u32[]{:S(2)}) copy-start(f32[96,192,128]{2,1,0:T(8,128)} %shard_map.46) | copy-start | bytes 28311556
  462.2 21.4 %collective-permute-start.4 = (f32[16,192,128]{2,1,0:T(8,128)S(1)}, f32[16,192,128]{2,1,0:T(8,128)S(1)}, u32[]{:S(2)}, u32[]{:S(2)}) collective-permute-start(f32[16,192,128]{2,1,0:T(8,128)S(1)} %get-tuple-element.58), channel_id=1, source_target_pairs={{0,8},{8,16},{16,24},{24,32},{32,40},{40,48},{48,56},{56,64},{64,7... | collective-permute-start | bytes 4718600 | tf_op jit(solution)/shard_map/ppermute | solution.py:38
  464.4 19.2 %slice-start.3 = ((f32[96,192,128]{2,1,0:T(8,128)}), f32[64,192,128]{2,1,0:T(8,128)S(1)}, s32[]{:S(2)}) async-start(f32[96,192,128]{2,1,0:T(8,128)} %shard_map.46), calls=%async_computation.3 | async-start | bytes 12582912 | tf_op jit(solution)/shard_map/slice | solution.py:189
  464.4 23.5 %collective-permute-start.5 = (f32[16,192,128]{2,1,0:T(8,128)S(1)}, f32[16,192,128]{2,1,0:T(8,128)S(1)}, u32[]{:S(2)}, u32[]{:S(2)}) collective-permute-start(f32[16,192,128]{2,1,0:T(8,128)S(1)} %get-tuple-element.57), channel_id=1, source_target_pairs={{8,0},{16,8},{24,16},{32,24},{40,32},{48,40},{56,48},{64,56},{72,6... | collective-permute-start | bytes 4718600 | tf_op jit(solution)/shard_map/ppermute | solution.py:38
  488.4 8.0 %collective-permute-start.6 = (f32[64,16,128]{2,1,0:T(8,128)S(1)}, f32[64,16,128]{2,1,0:T(8,128)S(1)}, u32[]{:S(2)}, u32[]{:S(2)}) collective-permute-start(f32[64,16,128]{2,1,0:T(8,128)S(1)} %get-tuple-element.60), channel_id=1, source_target_pairs={{0,1},{1,2},{2,3},{3,4},{4,5},{5,6},{6,7},{8,9},{9,10},{10,11},{11... | collective-permute-start | bytes 1572872 | tf_op jit(solution)/shard_map/ppermute | solution.py:38
  490.3 10.5 %collective-permute-start.7 = (f32[64,16,128]{2,1,0:T(8,128)S(1)}, f32[64,16,128]{2,1,0:T(8,128)S(1)}, u32[]{:S(2)}, u32[]{:S(2)}) collective-permute-start(f32[64,16,128]{2,1,0:T(8,128)S(1)} %get-tuple-element.59), channel_id=1, source_target_pairs={{1,0},{2,1},{3,2},{4,3},{5,4},{6,5},{7,6},{9,8},{10,9},{11,10},{12... | collective-permute-start | bytes 1572872 | tf_op jit(solution)/shard_map/ppermute | solution.py:38
  496.6 4.3 copy-start.4

commit v2 on v1

--- a/solution.py
+++ b/solution.py
@@ -38,48 +38,64 @@
     return lax.ppermute(x, axis, pairs)
 
 
-def subzone_kernel(spots_ref, count_ref, block_ref, total_ref,
+def subzone_kernel(spots_ref, count_ref, block_a, block_b, total_ref,
                    um_ref, mur_ref, muis_ref, w1_ref, w2_ref, t_ref,
                    img1_ref, s1_ref, v3_ref, p_ref, q_ref):
-    slot = pl.program_id(0)
-    lanes = block_ref.shape[-1]
+    step = pl.program_id(0)
+    lanes = block_a.shape[-1]
     half = lanes // 2
-
-    @pl.when(slot == 0)
+    group = half // 2
+    first = 2 * step
+    second = jnp.minimum(first + 1, count_ref[0] - 1)
+
+    @pl.when(step == 0)
     def _():
         total_ref[...] = jnp.zeros_like(total_ref)
         w1_ref[...] = jnp.zeros_like(w1_ref)
         w2_ref[...] = jnp.zeros_like(w2_ref)
         t_ref[...] = jnp.zeros_like(t_ref)
 
-    @pl.when(slot < count_ref[0])
+    @pl.when(first < count_ref[0])
     def _():
-        x0 = spots_ref[slot, 0]
-        y0 = pl.multiple_of(spots_ref[slot, 1], HALO)
-        z0 = spots_ref[slot, 2]
+        xa = spots_ref[first, 0]
+        ya = pl.multiple_of(spots_ref[first, 1], HALO)
+        za = spots_ref[first, 2]
+        xb = spots_ref[second, 0]
+        yb = pl.multiple_of(spots_ref[second, 1], HALO)
+        zb = spots_ref[second, 2]
         lane = lax.broadcasted_iota(jnp.int32, (SUB, lanes), 1)
         depth = lane % half
-        window = (depth >= z0) & (depth < z0 + SUB)
+        in_a = (lane % half) < group
         upper = lane >= half
+        not_low = (lane % group) != 0
+        not_high = (lane % group) != group - 1
+        shift_a = (lanes - za) % lanes
+        shift_b = (group - zb + lanes) % lanes
 
         def swap(v):
             return pltpu.roll(v, half, 1)
+
+        def packed(k, x):
+            a = block_a[k, x].astype(jnp.float32)
+            b = block_b[k, x].astype(jnp.float32)
+            return jnp.where(in_a, pltpu.roll(a, shift_a, 1), pltpu.roll(b, shift_b, 1))
 
         def laplace(ref, f, x):
             c = ref[f, x + 1, PADY:PADY + SUB, :]
             side = ref[f, x, PADY:PADY + SUB, :] + ref[f, x + 2, PADY:PADY + SUB, :]
             side = side + ref[f, x + 1, PADY - 1:PADY - 1 + SUB, :]
             side = side + ref[f, x + 1, PADY + 1:PADY + 1 + SUB, :]
-            side = side + pltpu.roll(c, 1, 1) + pltpu.roll(c, lanes - 1, 1)
+            side = side + jnp.where(not_low, pltpu.roll(c, 1, 1), 0.0)
+            side = side + jnp.where(not_high, pltpu.roll(c, lanes - 1, 1), 0.0)
             return 6.0 * c - side, c
 
         def stage_a(x, carry):
-            mu = jnp.where(window, block_ref[NF, x].astype(jnp.float32), 0.0)
+            mu = packed(NF, x)
             smu = swap(mu)
             mur_ref[x] = jnp.where(upper, smu, mu)
             muis_ref[x] = jnp.where(upper, mu, -smu)
             for f in range(NF):
-                u = jnp.where(window, block_ref[f, x].astype(jnp.float32), 0.0)
+                u = packed(f, x)
                 um_ref[f, x] = u
                 w1_ref[f, x + 1, PADY:PADY + SUB, :] = OMEGA * u
             return carry
@@ -121,6 +137,12 @@
 
         lax.fori_loop(0, SUB, stage_c, 0)
 
+        window_a = (depth >= za) & (depth < za + SUB)
+        window_b = (depth >= zb) & (depth < zb + SUB)
+        back_a = za % lanes
+        back_b = (zb + lanes - group) % lanes
+        live_b = first + 1 < count_ref[0]
+
         def stage_d(x, carry):
             pacc = p_ref[x]
             qacc = q_ref[x]
@@ -130,9 +152,13 @@
                 v2 = v3 - OMEGA * (v3 + lt)
                 pacc = pacc + v2 * img1_ref[f, x]
                 qacc = qacc + v2 * s1_ref[f, x]
-            res = jnp.where(upper, qacc - swap(qacc), pacc + swap(pacc))
-            res = jnp.where(window, -OMEGA * res, 0.0)
-            total_ref[x0 + x, pl.ds(y0, SUB), :] += res
+            res = -OMEGA * jnp.where(upper, qacc - swap(qacc), pacc + swap(pacc))
+            total_ref[xa + x, pl.ds(ya, SUB), :] += jnp.where(window_a, pltpu.roll(res, back_a, 1), 0.0)
+
+            @pl.when(live_b)
+            def _():
+                total_ref[xb + x, pl.ds(yb, SUB), :] += jnp.where(window_b, pltpu.roll(res, back_b, 1), 0.0)
+
             return carry
 
         lax.fori_loop(0, SUB, stage_d, 0)
@@ -143,16 +169,19 @@
     home = spots.shape[0]
     ex, ey = extended.shape[1], extended.shape[2]
 
-    def block_map(s, spots_ref, count_ref):
-        live = jnp.minimum(s, jnp.maximum(count_ref[0] - 1, 0))
-        return (0, spots_ref[live, 0], pl.multiple_of(spots_ref[live, 1], HALO), 0)
+    def block_map(offset):
+        def index(s, spots_ref, count_ref):
+            live = jnp.minimum(2 * s + offset, jnp.maximum(count_ref[0] - 1, 0))
+            return (0, spots_ref[live, 0], pl.multiple_of(spots_ref[live, 1], HALO), 0)
+        return index
 
     f32 = jnp.float32
     padded = (NF, SUB + 2, SUB + 2 * PADY, lanes)
+    block = (pl.Element(NF + 1), pl.Element(SUB), pl.Element(SUB), pl.Element(lanes))
     grid_spec = pltpu.PrefetchScalarGridSpec(
         num_scalar_prefetch=2,
-        grid=(home,),
-        in_specs=[pl.BlockSpec((pl.Element(NF + 1), pl.Element(SUB), pl.Element(SUB), pl.Element(lanes)), block_map)],
+        grid=((home + 1) // 2,),
+        in_specs=[pl.BlockSpec(block, block_map(0)), pl.BlockSpec(block, block_map(1))],
         out_specs=pl.BlockSpec((ex, ey, lanes), lambda s, spots_ref, count_ref: (0, 0, 0)),
         scratch_shapes=[
             pltpu.VMEM((NF, SUB, SUB, lanes), f32),
@@ -175,7 +204,7 @@
         compiler_params=pltpu.CompilerParams(
             dimension_semantics=("arbitrary",), vmem_limit_bytes=100 * 1024 * 1024
         ),
-    )(spots, count, extended)
+    )(spots, count, extended, extended)
 
 
 def shards(fields, modulus, anchors, home_count):

time: 510 us -> 388 us (0.76)
  Pallas kernels: 316 us -> 114 us
  starting transfers between devices: 22.6 us -> 101 us
    pallas_call x1, Pallas kernels: 316 us -> 114 us  [subzone_pass(): pl.pallas_call(subzone_kernel, grid_spec=grid_spec, out_shape=jax.ShapeDt...]
    ppermute x4, starting transfers between devices: 10.2 us -> 88.2 us  [passed_along(): return lax.ppermute(x, axis, pairs)]
where the time goes in v2:
time: 388 us; the launch traced here: 380 us
  waiting for transfers between devices  125 us (32%)
  Pallas kernels  114 us (29%)
  starting transfers between devices  101 us (26%)
  other arithmetic  35.8 us (9%)
    pallas_call x1, Pallas kernels, subzone_pass(): pl.pallas_call(subzone_kernel, grid_spec=grid_spec, out_shape=jax.ShapeDt...  114 us
    ppermute x4, starting transfers between devices, passed_along(): return lax.ppermute(x, axis, pairs)  88.2 us
    ppermute x2, waiting for transfers between devices, with_halo(): before = lax.ppermute(last, axis, up)  86.9 us
    ppermute x4, waiting for transfers between devices, passed_along(): return lax.ppermute(x, axis, pairs)  28.6 us
    concatenate x1, other arithmetic, with_halo(): x = jnp.concatenate([before, x, after], axis=dim)  26.8 us
    ppermute x2, waiting for transfers between devices, with_halo(): after = lax.ppermute(first, axis, down)  9.7 us
    ppermute x2, starting transfers between devices, with_halo(): before = lax.ppermute(last, axis, up)  8.61 us
  transfers between devices with their start and end apart: 8, of which 8 were waited for; matrix products, arithmetic and copies ran while one was open for 0% of the time, Pallas kernels for 0%

profile of v2, /device:TPU:7, one launch (start us, length us, event | category | flops | bytes accessed | tf_op | source)
XLA Modules:
  0.0 380.1 jit_solution(8417936236591187918)
XLA Ops:
  0.0 3.6 pad_maximum_fusion.2
  3.6 3.7 collective-permute-start
  7.4 1.9 collective-permute-start.1
  9.3 68.3 %collective-permute-done = bf16[5,16,160,128]{3,2,1,0:T(8,128)(2,1)S(1)} collective-permute-done((bf16[5,16,160,128]{3,2,1,0:T(8,128)(2,1)S(1)}, bf16[5,16,160,128]{3,2,1,0:T(8,128)(2,1)S(1)}, u32[]{:S(2)}, u32[]{:S(2)}) %collective-permute-start) | collective-permute-done | bytes 3276832 | tf_op jit(solution)/shard_map/ppermute | solution.py:29
  77.6 5.3 %collective-permute-done.1 = bf16[5,16,160,128]{3,2,1,0:T(8,128)(2,1)S(1)} collective-permute-done((bf16[5,16,160,128]{3,2,1,0:T(8,128)(2,1)S(1)}, bf16[5,16,160,128]{3,2,1,0:T(8,128)(2,1)S(1)}, u32[]{:S(2)}, u32[]{:S(2)}) %collective-permute-start.1) | collective-permute-done | bytes 3276832 | tf_op jit(solution)/shard_map/ppermute | solution.py:30
  82.9 2.9 pad_maximum_fusion.6
  85.8 4.9 %collective-permute-start.2 = (bf16[5,96,16,128]{3,2,1,0:T(8,128)(2,1)}, bf16[5,96,16,128]{3,2,1,0:T(8,128)(2,1)}, u32[]{:S(2)}, u32[]{:S(2)}) collective-permute-start(bf16[5,96,16,128]{3,2,1,0:T(8,128)(2,1)} %get-tuple-element.53), channel_id=1, source_target_pairs={{0,1},{1,2},{2,3},{3,4},{4,5},{5,6},{6,7},{8,9},{9,10},{10,11},{11... | collective-permute-start | bytes 5898248 | tf_op jit(solution)/shard_map/ppermute | solution.py:29
  90.7 1.9 collective-permute-start.3
  92.7 0.7 copy.6
  94.0 18.6 %collective-permute-done.2 = bf16[5,96,16,128]{3,2,1,0:T(8,128)(2,1)} collective-permute-done((bf16[5,96,16,128]{3,2,1,0:T(8,128)(2,1)}, bf16[5,96,16,128]{3,2,1,0:T(8,128)(2,1)}, u32[]{:S(2)}, u32[]{:S(2)}) %collective-permute-start.2) | collective-permute-done | bytes 1966112 | tf_op jit(solution)/shard_map/ppermute | solution.py:29
  112.6 4.4 %collective-permute-done.3 = bf16[5,96,16,128]{3,2,1,0:T(8,128)(2,1)} collective-permute-done((bf16[5,96,16,128]{3,2,1,0:T(8,128)(2,1)}, bf16[5,96,16,128]{3,2,1,0:T(8,128)(2,1)}, u32[]{:S(2)}, u32[]{:S(2)}) %collective-permute-start.3) | collective-permute-done | bytes 1966112 | tf_op jit(solution)/shard_map/ppermute | solution.py:30
  117.0 26.8 %pad_maximum_fusion.block_a.block_b = bf16[5,96,192,128]{3,2,1,0:T(8,128)(2,1)} fusion(bf16[5,96,16,128]{3,2,1,0:T(8,128)(2,1)} %collective-permute-done.3, bf16[5,16,160,128]{3,2,1,0:T(8,128)(2,1)} %copy-done.3, bf16[1,64,160,128]{3,2,1,0:T(8,128)(2,1)S(1)} %bitcast.8, bf16[4,64,160,128]{3,2,1,0:T(8,128)(2,1)} %param.12, ...), kind=kLoop, calls=%fused_computation | loop fusion | flops 141557760 | bytes 47185920 | tf_op jit(solution)/shard_map/concatenate | solution.py:31
  143.8 114.2 %shard_map.46 = f32[96,192,128]{2,1,0:T(8,128)} custom-call(s32[14,3]{1,0:T(8,128)} %bitcast.9, s32[1]{0:T(128)} %bitcast.3.count_ref, bf16[5,96,192,128]{3,2,1,0:T(8,128)(2,1)} %pad_maximum_fusion.block_a.block_b, bf16[5,96,192,128]{3,2,1,0:T(8,128)(2,1)} %pad_maximum_fusion.block_a.block_b), custom_call_target="tpu_custom_call" | custom-call | tf_op jit(solution)/shard_map/pallas_call | solution.py:200
  258.0 2.2 fusion.4
  260.3 81.5 %collective-permute-start.4 = (f32[16,192,128]{2,1,0:T(8,128)S(1)}, f32[16,192,128]{2,1,0:T(8,128)S(1)}, u32[]{:S(2)}, u32[]{:S(2)}) collective-permute-start(f32[16,192,128]{2,1,0:T(8,128)S(1)} %get-tuple-element.58), channel_id=1, source_target_pairs={{0,8},{8,16},{16,24},{24,32},{32,40},{40,48},{48,56},{56,64},{64,7... | collective-permute-start | bytes 4718600 | tf_op jit(solution)/shard_map/ppermute | solution.py:38
  341.8 2.3 collective-permute-start.5
  344.1 15.0 %collective-permute-done.4 = f32[16,192,128]{2,1,0:T(8,128)S(1)} collective-permute-done((f32[16,192,128]{2,1,0:T(8,128)S(1)}, f32[16,192,128]{2,1,0:T(8,128)S(1)}, u32[]{:S(2)}, u32[]{:S(2)}) %collective-permute-start.4) | collective-permute-done | bytes 1572896 | tf_op jit(solution)/shard_map/ppermute | solution.py:38
  359.3 6.0 %collective-permute-done.5 = f32[16,192,128]{2,1,0:T(8,128)S(1)} collective-permute-done((f32[16,192,128]{2,1,0:T(8,128)S(1)}, f32[16,192,128]{2,1,0:T(8,128)S(1)}, u32[]{:S(2)}, u32[]{:S(2)}) %collective-permute-start.5) | collective-permute-done | bytes 1572896 | tf_op jit(solution)/shard_map/ppermute | solution.py:38
  365.3 0.4 fusion
  365.8 1.9 collective-permute-start.6
  367.7 2.4 collective-permute-start.7
  370.5 3.3 collective-permute-done.6
  373.9 4.3 %collective-permute-done.7 = f32[64,16,128]{2,1,0:T(8,128)S(1)} collective-permute-done((f32[64,16,128]{2,1,0:T(8,128)S(1)}, f32[64,16,128]{2,1,0:T(8,128)S(1)}, u32[]{:S(2)}, u32[]{:S(2)}) %collective-permute-start.7) | collective-permute-done | bytes 524320 | tf_op jit(solution)/shard_map/ppermute | solution.py:38
  378.2 1.9 fusion.2
  (26 shorter events, 0.8 us)
Async XLA Ops:
  0.0 82.9 %slice-start = ((s8[10485760]{0:T(1024)(128)(4,1)}), s8[4194304]{0:T(1024)(128)(4,1)S(1)}, s32[]{:S(2)}) async-start(s8[10485760]{0:T(1024)(128)(4,1)} %bitcast.4), calls=%async_computation | async-start | bytes 8388608
  0.0 82.9 %slice-start.1 = ((s8[10485760]{0:T(1024)(128)(4,1)}), s8[4194304]{0:T(1024)(128)(4,1)S(1)}, s32[]{:S(2)}) async-start(s8[10485760]{0:T(1024)(128)(4,1)} %bitcast.4), calls=%async_computation.1 | async-start | bytes 8388608
  0.0 82.9 %slice-start.2 = ((s8[10485760]{0:T(1024)(128)(4,1)}), s8[2097152]{0:T(1024)(128)(4,1)S(1)}, s32[]{:S(2)}) async-start(s8[10485760]{0:T(1024)(128)(4,1)} %bitcast.4), calls=%async_computation.2 | async-start | bytes 4194304
  0.0 82.9 %copy-start.1 = (bf16[64,160,128]{2,1,0:T(8,128)(2,1)S(1)}, bf16[64,160,128]{2,1,0:T(8,128)(2,1)}, u32[]{:S(2)}) copy-start(bf16[64,160,128]{2,1,0:T(8,128)(2,1)} %param.13) | copy-start | bytes 7864324
  3.6 74.0 %collective-permute-start = (bf16[5,16,160,128]{3,2,1,0:T(8,128)(2,1)S(1)}, bf16[5,16,160,128]{3,2,1,0:T(8,128)(2,1)S(1)}, u32[]{:S(2)}, u32[]{:S(2)}) collective-permute-start(bf16[5,16,160,128]{3,2,1,0:T(8,128)(2,1)S(1)} %get-tuple-element.55), channel_id=1, source_target_pairs={{0,8},{8,16},{16,24},{24,32},{32,40},{40,48},{48,56},{56,64},{64,7... | collective-permute-start | bytes 9830408 | tf_op jit(solution)/shard_map/ppermute | solution.py:29
  7.3 85.3 %copy-start.5 = (s32[1,1,14,3]{2,1,3,0:T(1,128)S(1)}, s32[1,1,14,3]{2,1,3,0:T(1,128)}, u32[]{:S(2)}) copy-start(s32[1,1,14,3]{2,1,3,0:T(1,128)} %param.14) | copy-start | bytes 508
  7.4 75.5 %collective-permute-start.1 = (bf16[5,16,160,128]{3,2,1,0:T(8,128)(2,1)S(1)}, bf16[5,16,160,128]{3,2,1,0:T(8,128)(2,1)S(1)}, u32[]{:S(2)}, u32[]{:S(2)}) collective-permute-start(bf16[5,16,160,128]{3,2,1,0:T(8,128)(2,1)S(1)} %get-tuple-element.56), channel_id=1, source_target_pairs={{8,0},{16,8},{24,16},{32,24},{40,32},{48,40},{56,48},{64,56},{72,6... | collective-permute-start | bytes 9830408 | tf_op jit(solution)/shard_map/ppermute | solution.py:30
  77.6 8.2 %copy-start.2 = (bf16[5,16,160,128]{3,2,1,0:T(8,128)(2,1)}, bf16[5,16,160,128]{3,2,1,0:T(8,128)(2,1)S(1)}, u32[]{:S(2)}) copy-start(bf16[5,16,160,128]{3,2,1,0:T(8,128)(2,1)S(1)} %collective-permute-done) | copy-start | bytes 9830404
  82.9 2.9 copy-start.3
  85.8 26.8 %collective-permute-start.2 = (bf16[5,96,16,128]{3,2,1,0:T(8,128)(2,1)}, bf16[5,96,16,128]{3,2,1,0:T(8,128)(2,1)}, u32[]{:S(2)}, u32[]{:S(2)}) collective-permute-start(bf16[5,96,16,128]{3,2,1,0:T(8,128)(2,1)} %get-tuple-element.53), channel_id=1, source_target_pairs={{0,1},{1,2},{2,3},{3,4},{4,5},{5,6},{6,7},{8,9},{9,10},{10,11},{11... | collective-permute-start | bytes 5898248 | tf_op jit(solution)/shard_map/ppermute | solution.py:29
  90.7 26.3 %collective-permute-start.3 = (bf16[5,96,16,128]{3,2,1,0:T(8,128)(2,1)}, bf16[5,96,16,128]{3,2,1,0:T(8,128)(2,1)}, u32[]{:S(2)}, u32[]{:S(2)}) collective-permute-start(bf16[5,96,16,128]{3,2,1,0:T(8,128)(2,1)} %get-tuple-element.54), channel_id=1, source_target_pairs={{1,0},{2,1},{3,2},{4,3},{5,4},{6,5},{7,6},{9,8},{10,9},{11,10},{12... | collective-permute-start | bytes 5898248 | tf_op jit(solution)/shard_map/ppermute | solution.py:30
  258.0 101.1 %copy-start = (f32[96,192,128]{2,1,0:T(8,128)S(1)}, f32[96,192,128]{2,1,0:T(8,128)}, u32[]{:S(2)}) copy-start(f32[96,192,128]{2,1,0:T(8,128)} %shard_map.46) | copy-start | bytes 28311556
  260.3 98.8 %collective-permute-start.4 = (f32[16,192,128]{2,1,0:T(8,128)S(1)}, f32[16,192,128]{2,1,0:T(8,128)S(1)}, u32[]{:S(2)}, u32[]{:S(2)}) collective-permute-start(f32[16,192,128]{2,1,0:T(8,128)S(1)} %get-tuple-element.58), channel_id=1, source_target_pairs={{0,8},{8,16},{16,24},{24,32},{32,40},{40,48},{48,56},{56,64},{64,7... | collective-permute-start | bytes 4718600 | tf_op jit(solution)/shard_map/ppermute | solution.py:38
  341.7 17.3 %slice-start.3 = ((f32[96,192,128]{2,1,0:T(8,128)}), f32[64,192,128]{2,1,0:T(8,128)S(1)}, s32[]{:S(2)}) async-start(f32[96,192,128]{2,1,0:T(8,128)} %shard_map.46), calls=%async_computation.3 | async-start | bytes 12582912 | tf_op jit(solution)/shard_map/slice | solution.py:218
  341.8 23.5 %collective-permute-start.5 = (f32[16,192,128]{2,1,0:T(8,128)S(1)}, f32[16,192,128]{2,1,0:T(8,128)S(1)}, u32[]{:S(2)}, u32[]{:S(2)}) collective-permute-start(f32[16,192,128]{2,1,0:T(8,128)S(1)} %get-tuple-element.57), channel_id=1, source_target_pairs={{8,0},{16,8},{24,16},{32,24},{40,32},{48,40},{56,48},{64,56},{72,6... | collective-permute-start | bytes 4718600 | tf_op jit(solution)/shard_map/ppermute | solution.py:38
  365.8 8.0 %collective-permute-start.6 = (f32[64,16,128]{2,1,0:T(8,128)S(1)}, f32[64,16,128]{2,1,0:T(8,128)S(1)}, u32[]{:S(2)}, u32[]{:S(2)}) collective-permute-start(f32[64,16,128]{2,1,0:T(8,128)S(1)} %get-tuple-element.60), channel_id=1, source_target_pairs={{0,1},{1,2},{2,3},{3,4},{4,5},{5,6},{6,7},{8,9},{9,10},{10,11},{11... | collective-permute-start | bytes 1572872 | tf_op jit(solution)/shard_map/ppermute | solution.py:38
  367.7 10.5 %collective-permute-start.7 = (f32[64,16,128]{2,1,0:T(8,128)S(1)}, f32[64,16,128]{2,1,0:T(8,128)S(1)}, u32[]{:S(2)}, u32[]{:S(2)}) collective-permute-start(f32[64,16,128]{2,1,0:T(8,128)S(1)} %get-tuple-element.59), channel_id=1, source_target_pairs={{1,0},{2,1},{3,2},{4,3},{5,4},{6,5},{7,6},{9,8},{10,9},{11,10},{12... | collective-permute-start | bytes 1572872 | tf_op jit(solution)/shard_map/ppermute | solution.py:38
  373.9 4.3 %copy-start.4 = (f32[64,160,128]{2,1,0:T(8,128)}, f32[64,160,128]{2,1,0:T(8,128)S(1)}, u32[]{:S(2)}) copy-start(f32[64,160,128]{2,1,0:T(8,128)S(1)} %fusion.3) | copy-start | bytes 15728644

commit v3 on v2

--- a/solution.py
+++ b/solution.py
@@ -19,17 +19,32 @@
 PADY = 8
 
 
-def with_halo(x, sides, width):
-    for axis, dim in sides:
-        size, length = (lax.axis_size(axis), x.shape[dim])
-        up = [(i, (i + 1) % size) for i in range(size - 1)]
-        down = [(j, i) for i, j in up]
-        last = lax.slice_in_dim(x, length - width, length, axis=dim)
-        first = lax.slice_in_dim(x, 0, width, axis=dim)
-        before = lax.ppermute(last, axis, up)
-        after = lax.ppermute(first, axis, down)
-        x = jnp.concatenate([before, x, after], axis=dim)
-    return x
+def shifted(x, by_x, by_y):
+    nx, ny = lax.axis_size("vx"), lax.axis_size("vy")
+    pairs = []
+    for a in range(nx):
+        for b in range(ny):
+            if 0 <= a + by_x < nx and 0 <= b + by_y < ny:
+                pairs.append((a * ny + b, (a + by_x) * ny + b + by_y))
+    return lax.ppermute(x, ("vx", "vy"), pairs)
+
+
+def with_halo(x, width):
+    rows, cols = x.shape[1], x.shape[2]
+    top = x[:, rows - width :]
+    bottom = x[:, :width]
+    xlo = shifted(top, 1, 0)
+    xhi = shifted(bottom, -1, 0)
+    ylo = shifted(x[:, :, cols - width :], 0, 1)
+    yhi = shifted(x[:, :, :width], 0, -1)
+    c_ll = shifted(top[:, :, cols - width :], 1, 1)
+    c_lh = shifted(top[:, :, :width], 1, -1)
+    c_hl = shifted(bottom[:, :, cols - width :], -1, 1)
+    c_hh = shifted(bottom[:, :, :width], -1, -1)
+    left = jnp.concatenate([c_ll, ylo, c_hl], axis=1)
+    right = jnp.concatenate([c_lh, yhi, c_hh], axis=1)
+    middle = jnp.concatenate([xlo, x, xhi], axis=1)
+    return jnp.concatenate([left, middle, right], axis=2)
 
 
 def passed_along(x, axis, by):
@@ -38,7 +53,7 @@
     return lax.ppermute(x, axis, pairs)
 
 
-def subzone_kernel(spots_ref, count_ref, block_a, block_b, total_ref,
+def subzone_kernel(spots_ref, count_ref, block_a, mod_a, block_b, mod_b, total_ref,
                    um_ref, mur_ref, muis_ref, w1_ref, w2_ref, t_ref,
                    img1_ref, s1_ref, v3_ref, p_ref, q_ref):
     step = pl.program_id(0)
@@ -75,9 +90,9 @@
         def swap(v):
             return pltpu.roll(v, half, 1)
 
-        def packed(k, x):
-            a = block_a[k, x].astype(jnp.float32)
-            b = block_b[k, x].astype(jnp.float32)
+        def packed(ref_a, ref_b, k, x):
+            a = ref_a[k, x].astype(jnp.float32)
+            b = ref_b[k, x].astype(jnp.float32)
             return jnp.where(in_a, pltpu.roll(a, shift_a, 1), pltpu.roll(b, shift_b, 1))
 
         def laplace(ref, f, x):
@@ -90,12 +105,12 @@
             return 6.0 * c - side, c
 
         def stage_a(x, carry):
-            mu = packed(NF, x)
+            mu = packed(mod_a, mod_b, 0, x)
             smu = swap(mu)
             mur_ref[x] = jnp.where(upper, smu, mu)
             muis_ref[x] = jnp.where(upper, mu, -smu)
             for f in range(NF):
-                u = packed(f, x)
+                u = packed(block_a, block_b, f, x)
                 um_ref[f, x] = u
                 w1_ref[f, x + 1, PADY:PADY + SUB, :] = OMEGA * u
             return carry
@@ -164,24 +179,34 @@
         lax.fori_loop(0, SUB, stage_d, 0)
 
 
-def subzone_pass(extended, spots, count):
-    lanes = extended.shape[-1]
+def subzone_pass(fields, modulus, spots, count, shift, extent):
+    lanes = fields.shape[-1]
     home = spots.shape[0]
-    ex, ey = extended.shape[1], extended.shape[2]
-
-    def block_map(offset):
+    ex, ey = extent
+
+    def block_map(offset, base):
         def index(s, spots_ref, count_ref):
             live = jnp.minimum(2 * s + offset, jnp.maximum(count_ref[0] - 1, 0))
-            return (0, spots_ref[live, 0], pl.multiple_of(spots_ref[live, 1], HALO), 0)
+            row = jnp.clip(spots_ref[live, 0] - shift, 0, fields.shape[1] - SUB)
+            col = jnp.clip(spots_ref[live, 1] - shift, 0, fields.shape[2] - SUB)
+            col = pl.multiple_of(col, HALO)
+            return (base, row, col, 0)
         return index
 
     f32 = jnp.float32
     padded = (NF, SUB + 2, SUB + 2 * PADY, lanes)
-    block = (pl.Element(NF + 1), pl.Element(SUB), pl.Element(SUB), pl.Element(lanes))
+    block = (pl.Element(NF), pl.Element(SUB), pl.Element(SUB), pl.Element(lanes))
+    mod_block = (pl.Element(1), pl.Element(SUB), pl.Element(SUB), pl.Element(lanes))
+    base = modulus.shape[0] - 1
     grid_spec = pltpu.PrefetchScalarGridSpec(
         num_scalar_prefetch=2,
         grid=((home + 1) // 2,),
-        in_specs=[pl.BlockSpec(block, block_map(0)), pl.BlockSpec(block, block_map(1))],
+        in_specs=[
+            pl.BlockSpec(block, block_map(0, 0)),
+            pl.BlockSpec(mod_block, block_map(0, base)),
+            pl.BlockSpec(block, block_map(1, 0)),
+            pl.BlockSpec(mod_block, block_map(1, base)),
+        ],
         out_specs=pl.BlockSpec((ex, ey, lanes), lambda s, spots_ref, count_ref: (0, 0, 0)),
         scratch_shapes=[
             pltpu.VMEM((NF, SUB, SUB, lanes), f32),
@@ -204,15 +229,27 @@
         compiler_params=pltpu.CompilerParams(
             dimension_semantics=("arbitrary",), vmem_limit_bytes=100 * 1024 * 1024
         ),
-    )(spots, count, extended, extended)
+    )(spots, count, fields, modulus, fields, modulus)
 
 
 def shards(fields, modulus, anchors, home_count):
+    home = anchors.shape[2]
+    spots = (anchors[0, 0] * HALO).astype(jnp.int32)
+    count = home_count[0, 0].astype(jnp.int32)
+    slots = jnp.arange(home, dtype=jnp.int32)
+    live = slots < count
+    inner = (spots[:, 0] >= HALO) & (spots[:, 0] + SUB <= TX + HALO)
+    inner = inner & (spots[:, 1] >= HALO) & (spots[:, 1] + SUB <= TY + HALO) & live
+    order = jnp.argsort(jnp.where(inner, 0, 1).astype(jnp.int32), stable=True)
+    spots = spots[order]
+    first = (jnp.sum(inner.astype(jnp.int32)) // 2) * 2
+    rest = jnp.take(spots, (slots + first) % home, axis=0)
+    extent = (TX + 2 * HALO, TY + 2 * HALO)
+    inside = subzone_pass(fields, modulus[None], spots, first[None], HALO, extent)
     data = jnp.concatenate([fields, modulus[None]], axis=0)
-    extended = with_halo(data, (("vx", 1), ("vy", 2)), HALO)
-    spots = (anchors[0, 0] * HALO).astype(jnp.int32)
-    count = home_count[0].astype(jnp.int32)
-    total = subzone_pass(extended, spots, count)
+    extended = with_halo(data, HALO)
+    outside = subzone_pass(extended, extended, rest, (count - first)[None], 0, extent)
+    total = inside + outside
     from_above = passed_along(total[:HALO], "vx", -1)
     from_below = passed_along(total[TX + HALO :], "vx", 1)
     middle = total[HALO : HALO + TX]

time: 388 us -> 449 us (1.16)
  the two profiles are of different devices: /device:TPU:7 before, /device:TPU:86 now
where the time goes in v3:
time: 449 us; the launch traced here: 442 us
  waiting for transfers between devices  156 us (35%)
  Pallas kernels  150 us (33%)
  other arithmetic  75.2 us (17%)
  starting transfers between devices  52.3 us (12%)
  local copies, waits for them, and re-layouts  5.05 us (1%)
    pallas_call x2, Pallas kernels, subzone_pass(): pl.pallas_call(subzone_kernel, grid_spec=grid_spec, out_shape=jax.ShapeDt...  150 us
    ppermute x4, waiting for transfers between devices, passed_along(): return lax.ppermute(x, axis, pairs)  80.9 us
    ppermute x8, waiting for transfers between devices, shifted(): return lax.ppermute(x, ('vx', 'vy'), pairs)  74.9 us
    concatenate x1, other arithmetic, with_halo(): return jnp.concatenate([left, middle, right], axis=2)  47.6 us
    ppermute x4, starting transfers between devices, passed_along(): return lax.ppermute(x, axis, pairs)  27.8 us
    ppermute x8, starting transfers between devices, shifted(): return lax.ppermute(x, ('vx', 'vy'), pairs)  24.6 us
    add x1, other arithmetic, shards(): total = inside + outside  12.7 us
  transfers between devices with their start and end apart: 12, of which 7 were waited for; matrix products, arithmetic and copies ran while one was open for 2% of the time, Pallas kernels for 20%

profile of v3, /device:TPU:86, one launch (start us, length us, event | category | flops | bytes accessed | tf_op | source)
XLA Modules:
  0.0 441.6 jit_solution(5415393610937829745)
XLA Ops:
  0.0 5.6 %fusion = (bf16[5,16,160,128]{3,2,1,0:T(8,128)(2,1)}, bf16[5,16,160,128]{3,2,1,0:T(8,128)(2,1)}) fusion(bf16[4,64,160,128]{3,2,1,0:T(8,128)(2,1)} %block_b.1, bf16[1,64,160,128]{3,2,1,0:T(8,128)(2,1)} %bitcast.16), kind=kLoop, calls=%fused_computation.11 | loop fusion | flops 3276800 | bytes 19660800 | tf_op jit(solution)/shard_map/concatenate | solution.py:249
  5.6 3.7 collective-permute-start.3
  9.3 2.4 collective-permute-start.4
  12.9 4.6 %collective-permute-start = (bf16[5,16,16,128]{3,2,1,0:T(8,128)(2,1)S(1)}, bf16[5,16,16,128]{3,2,1,0:T(8,128)(2,1)}, u32[]{:S(2)}, u32[]{:S(2)}) collective-permute-start(bf16[5,16,16,128]{3,2,1,0:T(8,128)(2,1)S(1)} %get-tuple-element.57), channel_id=1, source_target_pairs={{0,9},{1,10},{2,11},{3,12},{4,13},{5,14},{6,15},{8,17},{9,18},{10,... | collective-permute-start | bytes 983048 | tf_op jit(solution)/shard_map/ppermute | solution.py:29
  17.5 2.1 pad_maximum_fusion
  19.6 3.9 collective-permute-start.1
  23.4 2.3 collective-permute-start.6
  27.0 59.8 %collective-permute-done = bf16[5,16,16,128]{3,2,1,0:T(8,128)(2,1)} collective-permute-done((bf16[5,16,16,128]{3,2,1,0:T(8,128)(2,1)S(1)}, bf16[5,16,16,128]{3,2,1,0:T(8,128)(2,1)}, u32[]{:S(2)}, u32[]{:S(2)}) %collective-permute-start) | collective-permute-done | bytes 327712 | tf_op jit(solution)/shard_map/ppermute | solution.py:29
  86.8 3.1 collective-permute-start.2
  93.8 7.7 %collective-permute-done.2 = bf16[5,16,16,128]{3,2,1,0:T(8,128)(2,1)S(1)} collective-permute-done((bf16[5,16,16,128]{3,2,1,0:T(8,128)(2,1)S(1)}, bf16[5,16,16,128]{3,2,1,0:T(8,128)(2,1)S(1)}, u32[]{:S(2)}, u32[]{:S(2)}) %collective-permute-start.2) | collective-permute-done | bytes 327712 | tf_op jit(solution)/shard_map/ppermute | solution.py:29
  101.6 2.8 collective-permute-start.5
  106.7 88.3 %shard_map.46 = f32[96,192,128]{2,1,0:T(8,128)} custom-call(s32[14,3]{1,0:T(8,128)} %copy-done.3, s32[1]{0:T(128)} %bitcast.2.count_ref, bf16[4,64,160,128]{3,2,1,0:T(8,128)(2,1)} %block_b.1, bf16[1,64,160,128]{3,2,1,0:T(8,128)(2,1)} %bitcast.17, bf16[4,64,160,128]{3,2,1,0:T(8,128)(2,1)} %block_b.1, bf16[1,64,160,128]{3,2,1,0:T(8,128)(2,1)} %bitcast.18), custom_call_target="tpu_custom_call" | custom-call | tf_op jit(solution)/shard_map/pallas_call | solution.py:225
  198.2 7.4 %collective-permute-done.7 = bf16[5,16,16,128]{3,2,1,0:T(8,128)(2,1)S(1)} collective-permute-done((bf16[5,16,16,128]{3,2,1,0:T(8,128)(2,1)}, bf16[5,16,16,128]{3,2,1,0:T(8,128)(2,1)S(1)}, u32[]{:S(2)}, u32[]{:S(2)}) %collective-permute-start.7) | collective-permute-done | bytes 327712 | tf_op jit(solution)/shard_map/ppermute | solution.py:29
  205.7 47.6 %maximum_maximum_fusion.block_a.mod_a.block_b.mod_b = bf16[5,96,192,128]{3,2,1,0:T(8,128)(2,1)} fusion(bf16[5,16,16,128]{3,2,1,0:T(8,128)(2,1)S(1)} %collective-permute-done.7, bf16[5,64,16,128]{3,2,1,0:T(8,128)(2,1)} %collective-permute-done.6, bf16[5,16,16,128]{3,2,1,0:T(8,128)(2,1)} %collective-permute-done.5, ...), kind=kLoop, calls=%fused_computation.6 | loop fusion | flops 235929600 | bytes 47185920 | tf_op jit(solution)/shard_map/concatenate | solution.py:47
  253.3 61.5 %shard_map.47 = f32[96,192,128]{2,1,0:T(8,128)} custom-call(s32[14,3]{1,0:T(8,128)} %broadcast_select_fusion.spots_ref, s32[1]{0:T(128)} %bitcast.5.count_ref, bf16[5,96,192,128]{3,2,1,0:T(8,128)(2,1)} %maximum_maximum_fusion.block_a.mod_a.block_b.mod_b, bf16[5,96,192,128]{3,2,1,0:T(8,128)(2,1)} %maximum_maximum_fusion.block_a.mod_a.block_b.mod_b, ...), custom_call_target="tpu_custom_call" | custom-call | tf_op jit(solution)/shard_map/pallas_call | solution.py:225
  314.9 12.7 %add.105 = f32[96,192,128]{2,1,0:T(8,128)} add(f32[96,192,128]{2,1,0:T(8,128)} %shard_map.46, f32[96,192,128]{2,1,0:T(8,128)} %shard_map.47) | non-fusion elementwise | flops 2359296 | bytes 28311552 | tf_op jit(solution)/shard_map/add | solution.py:252
  327.6 2.2 fusion.9
  329.9 2.2 collective-permute-start.8
  332.1 4.2 collective-permute-start.9
  336.2 29.6 %collective-permute-done.8 = f32[16,192,128]{2,1,0:T(8,128)S(1)} collective-permute-done((f32[16,192,128]{2,1,0:T(8,128)S(1)}, f32[16,192,128]{2,1,0:T(8,128)S(1)}, u32[]{:S(2)}, u32[]{:S(2)}) %collective-permute-start.8) | collective-permute-done | bytes 1572896 | tf_op jit(solution)/shard_map/ppermute | solution.py:53
  366.0 6.3 %collective-permute-done.9 = f32[16,192,128]{2,1,0:T(8,128)S(1)} collective-permute-done((f32[16,192,128]{2,1,0:T(8,128)S(1)}, f32[16,192,128]{2,1,0:T(8,128)S(1)}, u32[]{:S(2)}, u32[]{:S(2)}) %collective-permute-start.9) | collective-permute-done | bytes 1572896 | tf_op jit(solution)/shard_map/ppermute | solution.py:53
  374.7 19.5 %collective-permute-start.11 = (f32[64,16,128]{2,1,0:T(8,128)S(1)}, f32[64,16,128]{2,1,0:T(8,128)S(1)}, u32[]{:S(2)}, u32[]{:S(2)}) collective-permute-start(f32[64,16,128]{2,1,0:T(8,128)S(1)} %get-tuple-element.67), channel_id=1, source_target_pairs={{1,0},{2,1},{3,2},{4,3},{5,4},{6,5},{7,6},{9,8},{10,9},{11,10},{12... | collective-permute-start | bytes 1572872 | tf_op jit(solution)/shard_map/ppermute | solution.py:53
  394.6 4.6 %collective-permute-done.10 = f32[64,16,128]{2,1,0:T(8,128)S(1)} collective-permute-done((f32[64,16,128]{2,1,0:T(8,128)S(1)}, f32[64,16,128]{2,1,0:T(8,128)S(1)}, u32[]{:S(2)}, u32[]{:S(2)}) %collective-permute-start.10) | collective-permute-done | bytes 524320 | tf_op jit(solution)/shard_map/ppermute | solution.py:53
  399.2 40.4 %collective-permute-done.11 = f32[64,16,128]{2,1,0:T(8,128)S(1)} collective-permute-done((f32[64,16,128]{2,1,0:T(8,128)S(1)}, f32[64,16,128]{2,1,0:T(8,128)S(1)}, u32[]{:S(2)}, u32[]{:S(2)}) %collective-permute-start.11) | collective-permute-done | bytes 524320 | tf_op jit(solution)/shard_map/ppermute | solution.py:53
  (50 shorter events, 13.8 us)
Async XLA Ops:
  0.0 11.7 %slice-start = ((s8[10485760]{0:T(1024)(128)(4,1)}), s8[4194304]{0:T(1024)(128)(4,1)S(1)}, s32[]{:S(2)}) async-start(s8[10485760]{0:T(1024)(128)(4,1)} %bitcast.14), calls=%async_computation | async-start | bytes 8388608
  0.0 11.7 %slice-start.1 = ((s8[10485760]{0:T(1024)(128)(4,1)}), s8[4194304]{0:T(1024)(128)(4,1)S(1)}, s32[]{:S(2)}) async-start(s8[10485760]{0:T(1024)(128)(4,1)} %bitcast.14), calls=%async_computation.1 | async-start | bytes 8388608
  0.0 11.8 %slice-start.2 = ((s8[10485760]{0:T(1024)(128)(4,1)}), s8[2097152]{0:T(1024)(128)(4,1)S(1)}, s32[]{:S(2)}) async-start(s8[10485760]{0:T(1024)(128)(4,1)} %bitcast.14), calls=%async_computation.2 | async-start | bytes 4194304
  0.0 11.8 %copy-start = (bf16[64,160,128]{2,1,0:T(8,128)(2,1)S(1)}, bf16[64,160,128]{2,1,0:T(8,128)(2,1)}, u32[]{:S(2)}) copy-start(bf16[64,160,128]{2,1,0:T(8,128)(2,1)} %param.13) | copy-start | bytes 7864324
  5.6 200.0 %collective-permute-start.3 = (bf16[5,16,160,128]{3,2,1,0:T(8,128)(2,1)}, bf16[5,16,160,128]{3,2,1,0:T(8,128)(2,1)}, u32[]{:S(2)}, u32[]{:S(2)}) collective-permute-start(bf16[5,16,160,128]{3,2,1,0:T(8,128)(2,1)} %get-tuple-element.63), channel_id=1, source_target_pairs={{0,8},{1,9},{2,10},{3,11},{4,12},{5,13},{6,14},{7,15},{8,16},{9,17... | collective-permute-start | bytes 9830408 | tf_op jit(solution)/shard_map/ppermute | solution.py:29
  9.3 196.3 %collective-permute-start.4 = (bf16[5,16,160,128]{3,2,1,0:T(8,128)(2,1)}, bf16[5,16,160,128]{3,2,1,0:T(8,128)(2,1)}, u32[]{:S(2)}, u32[]{:S(2)}) collective-permute-start(bf16[5,16,160,128]{3,2,1,0:T(8,128)(2,1)} %get-tuple-element.64), channel_id=1, source_target_pairs={{8,0},{9,1},{10,2},{11,3},{12,4},{13,5},{14,6},{15,7},{16,8},{17,9... | collective-permute-start | bytes 9830408 | tf_op jit(solution)/shard_map/ppermute | solution.py:29
  12.9 12.8 %copy-start.5 = (s32[1,1,14,3]{2,1,3,0:T(1,128)S(1)}, s32[1,1,14,3]{2,1,3,0:T(1,128)}, u32[]{:S(2)}) copy-start(s32[1,1,14,3]{2,1,3,0:T(1,128)} %param.14) | copy-start | bytes 508
  12.9 73.9 %collective-permute-start = (bf16[5,16,16,128]{3,2,1,0:T(8,128)(2,1)S(1)}, bf16[5,16,16,128]{3,2,1,0:T(8,128)(2,1)}, u32[]{:S(2)}, u32[]{:S(2)}) collective-permute-start(bf16[5,16,16,128]{3,2,1,0:T(8,128)(2,1)S(1)} %get-tuple-element.57), channel_id=1, source_target_pairs={{0,9},{1,10},{2,11},{3,12},{4,13},{5,14},{6,15},{8,17},{9,18},{10,... | collective-permute-start | bytes 983048 | tf_op jit(solution)/shard_map/ppermute | solution.py:29
  19.6 186.1 %collective-permute-start.1 = (bf16[5,64,16,128]{3,2,1,0:T(8,128)(2,1)}, bf16[5,64,16,128]{3,2,1,0:T(8,128)(2,1)}, u32[]{:S(2)}, u32[]{:S(2)}) collective-permute-start(bf16[5,64,16,128]{3,2,1,0:T(8,128)(2,1)} %get-tuple-element.61), channel_id=1, source_target_pairs={{0,1},{1,2},{2,3},{3,4},{4,5},{5,6},{6,7},{8,9},{9,10},{10,11},{11... | collective-permute-start | bytes 3932168 | tf_op jit(solution)/shard_map/ppermute | solution.py:29
  23.4 182.2 %collective-permute-start.6 = (bf16[5,64,16,128]{3,2,1,0:T(8,128)(2,1)}, bf16[5,64,16,128]{3,2,1,0:T(8,128)(2,1)}, u32[]{:S(2)}, u32[]{:S(2)}) collective-permute-start(bf16[5,64,16,128]{3,2,1,0:T(8,128)(2,1)} %get-tuple-element.62), channel_id=1, source_target_pairs={{1,0},{2,1},{3,2},{4,3},{5,4},{6,5},{7,6},{9,8},{10,9},{11,10},{12... | collective-permute-start | bytes 3932168 | tf_op jit(solution)/shard_map/ppermute | solution.py:29
  86.8 14.8 %collective-permute-start.2 = (bf16[5,16,16,128]{3,2,1,0:T(8,128)(2,1)S(1)}, bf16[5,16,16,128]{3,2,1,0:T(8,128)(2,1)S(1)}, u32[]{:S(2)}, u32[]{:S(2)}) collective-permute-start(bf16[5,16,16,128]{3,2,1,0:T(8,128)(2,1)S(1)} %get-tuple-element.60), channel_id=1, source_target_pairs={{8,1},{9,2},{10,3},{11,4},{12,5},{13,6},{14,7},{16,9},{17,10},{18,... | collective-permute-start | bytes 983048 | tf_op jit(solution)/shard_map/ppermute | solution.py:29
  101.6 5.1 %copy-start.4 = (bf16[5,16,16,128]{3,2,1,0:T(8,128)(2,1)}, bf16[5,16,16,128]{3,2,1,0:T(8,128)(2,1)S(1)}, u32[]{:S(2)}) copy-start(bf16[5,16,16,128]{3,2,1,0:T(8,128)(2,1)S(1)} %collective-permute-done.2) | copy-start | bytes 983044
  101.6 93.4 %collective-permute-start.5 = (bf16[5,16,16,128]{3,2,1,0:T(8,128)(2,1)}, bf16[5,16,16,128]{3,2,1,0:T(8,128)(2,1)}, u32[]{:S(2)}, u32[]{:S(2)}) collective-permute-start(bf16[5,16,16,128]{3,2,1,0:T(8,128)(2,1)} %get-tuple-element.58), channel_id=1, source_target_pairs={{1,8},{2,9},{3,10},{4,11},{5,12},{6,13},{7,14},{9,16},{10,17},{11,... | collective-permute-start | bytes 983048 | tf_op jit(solution)/shard_map/ppermute | solution.py:29
  104.9 0.6 copy-start.3
  194.9 10.7 %collective-permute-start.7 = (bf16[5,16,16,128]{3,2,1,0:T(8,128)(2,1)}, bf16[5,16,16,128]{3,2,1,0:T(8,128)(2,1)S(1)}, u32[]{:S(2)}, u32[]{:S(2)}) collective-permute-start(bf16[5,16,16,128]{3,2,1,0:T(8,128)(2,1)} %get-tuple-element.59), channel_id=1, source_target_pairs={{9,0},{10,1},{11,2},{12,3},{13,4},{14,5},{15,6},{17,8},{18,9},{19,... | collective-permute-start | bytes 983048 | tf_op jit(solution)/shard_map/ppermute | solution.py:29
  327.6 38.2 %copy-start.1 = (f32[96,192,128]{2,1,0:T(8,128)S(1)}, f32[96,192,128]{2,1,0:T(8,128)}, u32[]{:S(2)}) copy-start(f32[96,192,128]{2,1,0:T(8,128)} %add.105) | copy-start | bytes 28311556
  329.9 36.0 %collective-permute-start.8 = (f32[16,192,128]{2,1,0:T(8,128)S(1)}, f32[16,192,128]{2,1,0:T(8,128)S(1)}, u32[]{:S(2)}, u32[]{:S(2)}) collective-permute-start(f32[16,192,128]{2,1,0:T(8,128)S(1)} %get-tuple-element.66), channel_id=1, source_target_pairs={{0,8},{8,16},{16,24},{24,32},{32,40},{40,48},{48,56},{56,64},{64,7... | collective-permute-start | bytes 4718600 | tf_op jit(solution)/shard_map/ppermute | solution.py:53
  332.0 33.8 %slice-start.3 = ((f32[96,192,128]{2,1,0:T(8,128)}), f32[64,192,128]{2,1,0:T(8,128)S(1)}, s32[]{:S(2)}) async-start(f32[96,192,128]{2,1,0:T(8,128)} %add.105), calls=%async_computation.3 | async-start | bytes 12582912 | tf_op jit(solution)/shard_map/slice | solution.py:255
  332.1 40.3 %collective-permute-start.9 = (f32[16,192,128]{2,1,0:T(8,128)S(1)}, f32[16,192,128]{2,1,0:T(8,128)S(1)}, u32[]{:S(2)}, u32[]{:S(2)}) collective-permute-start(f32[16,192,128]{2,1,0:T(8,128)S(1)} %get-tuple-element.65), channel_id=1, source_target_pairs={{8,0},{16,8},{24,16},{32,24},{40,32},{48,40},{56,48},{64,56},{72,6... | collective-permute-start | bytes 4718600 | tf_op jit(solution)/shard_map/ppermute | solution.py:53
  372.8 26.3 %collective-permute-start.10 = (f32[64,16,128]{2,1,0:T(8,128)S(1)}, f32[64,16,128]{2,1,0:T(8,128)S(1)}, u32[]{:S(2)}, u32[]{:S(2)}) collective-permute-start(f32[64,16,128]{2,1,0:T(8,128)S(1)} %get-tuple-element.68), channel_id=1, source_target_pairs={{0,1},{1,2},{2,3},{3,4},{4,5},{5,6},{6,7},{8,9},{9,10},{10,11},{11... | collective-permute-start | bytes 1572872 | tf_op jit(solution)/shard_map/ppermute | solution.py:53
  374.7 64.9 %collective-permute-start.11 = (f32[64,16,128]{2,1,0:T(8,128)S(1)}, f32[64,16,128]{2,1,0:T(8,128)S(1)}, u32[]{:S(2)}, u32[]{:S(2)}) collective-permute-start(f32[64,16,128]{2,1,0:T(8,128)S(1)} %get-tuple-element.67), channel_id=1, source_target_pairs={{1,0},{2,1},{3,2},{4,3},{5,4},{6,5},{7,6},{9,8},{10,9},{11,10},{12... | collective-permute-start | bytes 1572872 | tf_op jit(solution)/shard_map/ppermute | solution.py:53
  399.2 40.4 %copy-start.2 = (f32[64,160,128]{2,1,0:T(8,128)}, f32[64,160,128]{2,1,0:T(8,128)S(1)}, u32[]{:S(2)}) copy-start(f32[64,160,128]{2,1,0:T(8,128)S(1)} %fusion.6) | copy-start | bytes 15728644
